TPU v7x, 32 devices: a whole 2x2x4 slice. The times are simulated.
32 devices in a mesh: dp: 8 (over z, y), feat: 4 (over x, core).
Axes of the slice: x: 2, y: 2, z: 4, core: 2. Of those that a mesh axis runs over, the one named last changes fastest.
Arguments:
- activations: bfloat16 [16384, 2048], P('feat', 'dp'), may hold values from -6 to 6
- cotangent: bfloat16 [16384, 2048], P('feat', 'dp'), may hold values from -6 to 6
- r_mix: bfloat16 [64, 256, 256], P('feat', 'dp'), may hold values from -0.375 to 0.375
- l_mix: bfloat16 [256, 4096], P('feat', 'dp'), may hold values from -0.75 to 0.75
Outputs:
- grad_x: bfloat16 [16384, 2048], P('feat', 'dp')
- grad_r: float32 [64, 256, 256], P('feat', 'dp')
- grad_l: float32 [256, 4096], P('feat', 'dp')
All inputs are finite; a program needn't handle non-finite values.
Results may differ from a plain program's by a relative error of at most 0.0055.
Values may be sent and summed in bfloat16 or wider, within the bound.
No kernel may reach another device: no remote copies, remote signals or barrier semaphores. Data moves between devices by JAX's collectives and lax.ppermute only.
A program may use at most 64 MiB of HBM per device.

v0:
```python
import math
import jax
import jax.numpy as jnp
import numpy as np
from jax import lax
from jax.sharding import PartitionSpec as P

BLOCKS = 64
WIDTH = 256


def gelu_tanh(values):
    return jax.nn.gelu(values, approximate=True)


def slope_of(pre_act, upstream):
    _, pullback = jax.vjp(gelu_tanh, pre_act)
    return pullback(upstream.astype(jnp.float32))[0].astype(jnp.bfloat16)


def ring_of(mesh):
    row = mesh.devices[(slice(None),) + (0,) * (mesh.devices.ndim - 1)]
    size = len(row)
    try:
        spots = [tuple(d.coords) for d in row]
    except AttributeError:
        return list(range(size))
    near = [
        [j for j in range(size) if sum((abs(a - b) for a, b in zip(spots[i], spots[j]))) == 1]
        for i in range(size)
    ]
    path, seen, budget = ([0], {0}, [20000])

    def grow():
        budget[0] -= 1
        if budget[0] < 0:
            return False
        if len(path) == size:
            return 0 in near[path[-1]] or size <= 2
        here = path[-1]
        for nxt in sorted(near[here], key=lambda j: len([k for k in near[j] if k not in seen])):
            if nxt in seen:
                continue
            path.append(nxt)
            seen.add(nxt)
            if grow():
                return True
            path.pop()
            seen.discard(nxt)
        return False

    return list(path) if grow() else list(range(size))


def ring_reduce_scatter(parts, ring):
    n = len(ring)
    order = jnp.asarray(np.array(ring, np.int32))
    place = jnp.asarray(np.argsort(np.array(ring)).astype(np.int32))
    here = place[lax.axis_index("dp")]
    half = parts.shape[1] // 2
    halves = (parts[:, :half], parts[:, half:])
    forward = [(ring[p], ring[(p + 1) % n]) for p in range(n)]
    backward = [(ring[p], ring[(p - 1) % n]) for p in range(n)]
    totals = []
    for way, pairs, src in ((1, forward, halves[0]), (-1, backward, halves[1])):
        acc = None
        for step in range(n):
            owner = order[(here - way * (1 + step)) % n]
            mine = lax.dynamic_index_in_dim(src, owner, axis=0, keepdims=False)
            acc = mine if acc is None else acc + mine
            if step < n - 1:
                acc = lax.ppermute(acc, "dp", pairs)
        totals.append(acc)
    return jnp.concatenate(totals, axis=0)


def body(ring, activations, cotangent, r_mix, l_mix):
    tok_count = activations.shape[1]
    local_blocks = activations.shape[0] // WIDTH
    n_dp = lax.axis_size("dp")
    grad_scale = 1.0 / math.sqrt(tok_count * n_dp)
    x_blocks = activations.reshape(local_blocks, WIDTH, tok_count)
    g_blocks = cotangent.reshape(local_blocks, WIDTH, tok_count)
    g_cols = lax.all_to_all(g_blocks, "feat", split_axis=1, concat_axis=0, tiled=True)
    local_cols = l_mix.shape[0]
    rows_r = r_mix.shape[1]
    r_flat = r_mix.reshape(1, -1)
    packed = jnp.concatenate([r_flat, l_mix.reshape(1, -1)], axis=1)
    packed = lax.all_gather(packed, "dp", axis=0, tiled=True)
    r_size = r_flat.shape[1]
    r_whole = packed[:, :r_size].reshape(n_dp, local_blocks, rows_r, WIDTH)
    r_whole = jnp.transpose(r_whole, (1, 0, 2, 3)).reshape(local_blocks, n_dp * rows_r, WIDTH)
    l_whole = packed[:, r_size:].reshape(n_dp, local_cols, -1, BLOCKS)
    l_blocks = jnp.transpose(l_whole, (0, 2, 1, 3)).reshape(-1, local_cols, BLOCKS)
    mixed_rows = jnp.einsum(
        "bit,bio->bot", x_blocks, r_whole, preferred_element_type=jnp.float32
    ).astype(jnp.bfloat16)
    columns = lax.all_to_all(mixed_rows, "feat", split_axis=1, concat_axis=0, tiled=True)
    pre_act = jnp.einsum("bst,bsc->cst", columns, l_blocks, preferred_element_type=jnp.float32)
    slope_cols = slope_of(pre_act, g_cols)
    back_cols = jnp.einsum(
        "cst,bsc->sbt", slope_cols, l_blocks, preferred_element_type=jnp.float32
    ).astype(jnp.bfloat16)
    l_term = jnp.einsum("bst,cst->bsc", columns, slope_cols, preferred_element_type=jnp.float32)
    l_term = (l_term * grad_scale).reshape(n_dp, -1, local_cols, BLOCKS)
    grad_l = ring_reduce_scatter(l_term, ring)
    grad_l = jnp.transpose(grad_l, (1, 0, 2)).reshape(local_cols, -1)
    back_rows = lax.all_to_all(back_cols, "feat", split_axis=1, concat_axis=0, tiled=True)
    through_r = jnp.einsum("obt,bio->bit", back_rows, r_whole, preferred_element_type=jnp.float32)
    grad_x = (
        (g_blocks.astype(jnp.float32) + through_r)
        .astype(jnp.bfloat16)
        .reshape(local_blocks * WIDTH, tok_count)
    )
    r_term = (
        jnp.einsum("bit,obt->ibo", x_blocks, back_rows, preferred_element_type=jnp.float32)
        * grad_scale
    ).reshape(n_dp, rows_r, local_blocks, WIDTH)
    grad_r = ring_reduce_scatter(r_term, ring)
    grad_r = jnp.transpose(grad_r, (1, 0, 2))
    return (grad_x, grad_r, grad_l)


def solution(mesh):
    ring = ring_of(mesh)
    placed = (P("feat", "dp"), P("feat", "dp"), P("feat", "dp", None), P("feat", "dp"))
    return jax.shard_map(
        lambda *args: body(ring, *args),
        mesh=mesh,
        in_specs=placed,
        out_specs=(P("feat", "dp"), P("feat", "dp", None), P("feat", "dp")),
        check_vma=False,
    )
```

profile of v0, /device:TPU:0, one launch (start us, length us, event | category | flops | bytes accessed | tf_op | source)
XLA Modules:
  0.0 299.4 jit_solution(11265219353165768789)
XLA Ops:
  7.2 1.1 copy.50
  8.3 1.0 reshape.111
  9.4 3.6 %maximum_bitcast_fusion = bf16[1,1,163840]{2,1,0:T(2,128)(2,1)} fusion(bf16[1,32768]{1,0:T(2,128)(2,1)S(1)} %bitcast.189, bf16[1,131072]{1,0:T(2,128)(2,1)S(1)} %reshape.111), kind=kLoop, calls=%fused_computation.22 | loop fusion | flops 655360 | bytes 655360
  13.0 4.1 %copy.37 = bf16[16,256,256]{2,0,1:T(8,128)(2,1)} copy(bf16[16,256,256]{2,1,0:T(8,128)(2,1)} %bitcast.183) | data formatting | bytes 4194304 | tf_op jit(solution)/shard_map/reshape | solution.py:83
  17.1 4.5 %all-to-all-start = ((bf16[16,256,256]{2,0,1:T(8,128)(2,1)}), bf16[16,256,256]{2,0,1:T(8,128)(2,1)}, u32[]{:S(2)}, u32[]{:S(2)}) async-start(bf16[16,256,256]{2,0,1:T(8,128)(2,1)} %copy.37), calls=%async_computation | async-start | bytes 4194304 | tf_op jit(solution)/shard_map/all_to_all | solution.py:84
  21.6 80.6 %all-gather.3.cloned.1.call-done = bf16[8,1,163840]{2,1,0:T(2,128)(2,1)} async-done(((bf16[1,1,163840]{2,1,0:T(2,128)(2,1)}), bf16[8,1,163840]{2,1,0:T(2,128)(2,1)}) %all-gather.3.cloned.1.call-update) | async-done | bytes 2621456 | tf_op jit(solution)/shard_map/all_gather | solution.py:89
  102.1 5.8 %copy.58 = bf16[8,1,163840]{2,0,1:T(8,128)(2,1)S(1)} copy(bf16[8,1,163840]{2,1,0:T(2,128)(2,1)} %all-gather.3.cloned.1.call-done) | data formatting | bytes 5242880
  108.1 1.4 copy-done.3
  111.5 2.5 copy.40
  114.0 4.8 %all-to-all-start.1 = ((bf16[16,256,256]{2,0,1:T(8,128)(2,1)}), bf16[16,256,256]{2,0,1:T(8,128)(2,1)}, u32[]{:S(2)}, u32[]{:S(2)}) async-start(bf16[16,256,256]{2,0,1:T(8,128)(2,1)} %copy.40), calls=%async_computation.1 | async-start | bytes 4194304 | tf_op jit(solution)/shard_map/all_to_all | solution.py:98
  160.8 4.2 %copy.38 = f32[16,4,64,256]{3,0,1,2:T(8,128)} copy(bf16[16,4,64,256]{3,0,2,1:T(8,128)(2,1)} %bitcast.92) | data formatting | bytes 6291456 | tf_op jit(solution)/shard_map/convert_element_type | solution.py:18
  164.9 1.1 slice.25
  166.0 2.1 reshape.115
  168.1 1.5 copy.36
  169.6 2.0 copy.41
  172.4 5.1 %fusion.6 = bf16[64,64,256]{2,0,1:T(8,128)(2,1)S(1)} fusion(f32[16,4,64,256]{3,0,1,2:T(8,128)S(1)} %copy-done.6, bf16[64,64,256]{2,0,1:T(8,128)(2,1)S(1)} %bitcast.179, bf16[64,64,64]{2,1,0:T(8,128)(2,1)S(1)} %bitcast.185), kind=kOutput, calls=%fused_computation.8 | convolution fusion | flops 155189248 | bytes 8912896 | tf_op jit(solution)/shard_map/bst,bsc->cst/dot_general | solution.py:99
  177.5 2.0 multiply_bitcast_fusion
  179.5 1.3 convolution_convert_fusion
  180.8 2.5 copy.44
  183.4 3.8 %copy.46 = f32[64,64,64]{2,1,0:T(8,128)} copy(f32[64,64,64]{0,2,1:T(8,128)} %multiply_bitcast_fusion) | data formatting | bytes 2097152 | tf_op jit(solution)/shard_map/mul | solution.py:105
  187.2 2.7 fusion.13
  189.9 4.5 %all-to-all-start.2 = ((bf16[64,64,256]{2,0,1:T(8,128)(2,1)}), bf16[64,64,256]{2,0,1:T(8,128)(2,1)}, u32[]{:S(2)}, u32[]{:S(2)}) async-start(bf16[64,64,256]{2,0,1:T(8,128)(2,1)} %copy.44), calls=%async_computation.2 | async-start | bytes 4194304 | tf_op jit(solution)/shard_map/all_to_all | solution.py:108
  194.3 0.9 dynamic-slice_bitcast_fusion.2
  195.7 1.7 collective-permute-start.14
  197.4 3.8 %collective-permute-done.21 = f32[4,64,64]{2,1,0:T(8,128)S(1)} collective-permute-done((f32[4,64,64]{2,1,0:T(8,128)S(1)}, f32[4,64,64]{2,1,0:T(8,128)S(1)}, u32[]{:S(2)}, u32[]{:S(2)}) %collective-permute-start.21) | collective-permute-done | bytes 65568 | tf_op jit(solution)/shard_map/ppermute | solution.py:72
  201.2 0.9 bitcast_add_fusion.20
  202.6 1.7 collective-permute-start.15
  204.3 3.1 %collective-permute-done.22 = f32[4,64,64]{2,1,0:T(8,128)S(1)} collective-permute-done((f32[4,64,64]{2,1,0:T(8,128)S(1)}, f32[4,64,64]{2,1,0:T(8,128)S(1)}, u32[]{:S(2)}, u32[]{:S(2)}) %collective-permute-start.22) | collective-permute-done | bytes 65568 | tf_op jit(solution)/shard_map/ppermute | solution.py:72
  207.3 0.9 bitcast_add_fusion.19
  208.7 1.7 collective-permute-start.16
  210.4 2.9 collective-permute-done.23
  213.3 0.9 bitcast_add_fusion.18
  214.7 1.7 collective-permute-start.17
  216.4 2.9 collective-permute-done.24
  219.2 0.9 bitcast_add_fusion.17
  220.6 1.7 collective-permute-start.18
  222.3 2.9 collective-permute-done.25
  225.2 0.9 bitcast_add_fusion.16
  226.6 1.8 copy.45
  230.5 1.7 collective-permute-start.7
  232.6 0.9 bitcast_add_fusion.23
  233.5 1.7 collective-permute-start.19
  235.2 2.4 collective-permute-done.7
  237.7 2.6 collective-permute-start.8
  240.5 0.9 bitcast_add_fusion.15
  241.4 2.1 collective-permute-start.27
  243.5 3.2 %collective-permute-done.8 = f32[16,16,256]{2,0,1:T(8,128)S(1)} collective-permute-done((f32[16,16,256]{2,0,1:T(8,128)S(1)}, f32[16,16,256]{2,0,1:T(8,128)S(1)}, u32[]{:S(2)}, u32[]{:S(2)}) %collective-permute-start.8) | collective-permute-done | bytes 262176 | tf_op jit(solution)/shard_map/ppermute | solution.py:72
  246.8 2.5 collective-permute-start.9
  249.4 1.6 collective-permute-start.20
  251.0 4.7 %collective-permute-done.9 = f32[16,16,256]{2,0,1:T(8,128)S(1)} collective-permute-done((f32[16,16,256]{2,0,1:T(8,128)S(1)}, f32[16,16,256]{2,0,1:T(8,128)S(1)}, u32[]{:S(2)}, u32[]{:S(2)}) %collective-permute-start.9) | collective-permute-done | bytes 262176 | tf_op jit(solution)/shard_map/ppermute | solution.py:72
  255.8 2.5 collective-permute-start.10
  258.5 0.9 bitcast_add_fusion.14
  259.4 5.3 %collective-permute-done.10 = f32[16,16,256]{2,0,1:T(8,128)S(1)} collective-permute-done((f32[16,16,256]{2,0,1:T(8,128)S(1)}, f32[16,16,256]{2,0,1:T(8,128)S(1)}, u32[]{:S(2)}, u32[]{:S(2)}) %collective-permute-start.10) | collective-permute-done | bytes 262176 | tf_op jit(solution)/shard_map/ppermute | solution.py:72
  264.7 1.7 collective-permute-start.11
  266.9 5.8 %collective-permute-done.11 = f32[16,16,256]{2,0,1:T(8,128)S(1)} collective-permute-done((f32[16,16,256]{2,0,1:T(8,128)S(1)}, f32[16,16,256]{2,0,1:T(8,128)S(1)}, u32[]{:S(2)}, u32[]{:S(2)}) %collective-permute-start.11) | collective-permute-done | bytes 262176 | tf_op jit(solution)/shard_map/ppermute | solution.py:72
  272.7 1.0 collective-permute-start.12
  273.8 1.1 collective-permute-start.5
  275.9 4.9 %collective-permute-done.12 = f32[16,16,256]{2,0,1:T(8,128)S(1)} collective-permute-done((f32[16,16,256]{2,0,1:T(8,128)S(1)}, f32[16,16,256]{2,0,1:T(8,128)S(1)}, u32[]{:S(2)}, u32[]{:S(2)}) %collective-permute-start.12) | collective-permute-done | bytes 262176 | tf_op jit(solution)/shard_map/ppermute | solution.py:72
  280.7 1.0 bitcast_add_fusion.1
  282.1 1.0 bitcast_add_fusion.8
  283.1 1.8 collective-permute-start.6
  284.9 4.9 %add_convert_fusion = bf16[16,256,256]{2,1,0:T(8,128)(2,1)} fusion(bf16[16,256,256]{2,1,0:T(8,128)(2,1)} %bitcast.184, bf16[16,256,256]{2,1,0:T(8,128)(2,1)} %bitcast.173, bf16[256,16,256]{2,0,1:T(8,128)(2,1)} %bitcast.175), kind=kOutput, calls=%fused_computation.14 | convolution fusion | flops 540016640 | bytes 8388608 | tf_op jit(solution)/shard_map/obt,bio->bit/dot_general | solution.py:109
  289.8 1.0 bitcast_add_fusion
  290.8 1.0 bitcast_add_fusion.7
  (81 shorter events, 12.8 us)
Async XLA Ops:
  7.2 102.9 %copy-start = (bf16[4096,256]{1,0:T(8,128)(2,1)S(1)}, bf16[4096,256]{1,0:T(8,128)(2,1)}, u32[]{:S(2)}) copy-start(bf16[4096,256]{1,0:T(8,128)(2,1)} %param.8) | copy-start | bytes 6291460
  7.2 94.9 %all-gather.3.cloned.1.call-start = ((), (), s32[]{:S(2)}) async-start(), calls=%async_computation.3 | async-start | bytes 5898240 | tf_op jit(solution)/shard_map/all_gather | solution.py:89
  17.1 96.9 %all-to-all-start = ((bf16[16,256,256]{2,0,1:T(8,128)(2,1)}), bf16[16,256,256]{2,0,1:T(8,128)(2,1)}, u32[]{:S(2)}, u32[]{:S(2)}) async-start(bf16[16,256,256]{2,0,1:T(8,128)(2,1)} %copy.37), calls=%async_computation | async-start | bytes 4194304 | tf_op jit(solution)/shard_map/all_to_all | solution.py:84
  108.0 1.5 copy-start.3
  110.1 1.4 copy-start.1
  114.0 4.8 %copy-start.8 = (s32[8]{0:T(128)S(1)}, s32[8]{0:T(128)}, u32[]{:S(2)}) copy-start(s32[8]{0:T(128)} %constant.327.clone) | copy-start | bytes 100
  114.0 16.1 %copy-start.7 = (s32[8]{0:T(128)S(1)}, s32[8]{0:T(128)}, u32[]{:S(2)}) copy-start(s32[8]{0:T(128)} %constant.326.clone) | copy-start | bytes 100
  114.0 55.6 %all-to-all-start.1 = ((bf16[16,256,256]{2,0,1:T(8,128)(2,1)}), bf16[16,256,256]{2,0,1:T(8,128)(2,1)}, u32[]{:S(2)}, u32[]{:S(2)}) async-start(bf16[16,256,256]{2,0,1:T(8,128)(2,1)} %copy.40), calls=%async_computation.1 | async-start | bytes 4194304 | tf_op jit(solution)/shard_map/all_to_all | solution.py:98
  169.6 2.8 copy-start.6
  189.9 36.7 %all-to-all-start.2 = ((bf16[64,64,256]{2,0,1:T(8,128)(2,1)}), bf16[64,64,256]{2,0,1:T(8,128)(2,1)}, u32[]{:S(2)}, u32[]{:S(2)}) async-start(bf16[64,64,256]{2,0,1:T(8,128)(2,1)} %copy.44), calls=%async_computation.2 | async-start | bytes 4194304 | tf_op jit(solution)/shard_map/all_to_all | solution.py:108
  195.3 5.9 %collective-permute-start.21 = (f32[4,64,64]{2,1,0:T(8,128)S(1)}, f32[4,64,64]{2,1,0:T(8,128)S(1)}, u32[]{:S(2)}, u32[]{:S(2)}) collective-permute-start(f32[4,64,64]{2,1,0:T(8,128)S(1)} %dynamic-slice_bitcast_fusion.2), channel_id=1, source_target_pairs={{0,8},{4,0},{12,4},{20,12},{28,20},{24,28},{16,24},{8,16},{1,9},{5... | collective-permute-start | bytes 196616 | tf_op jit(solution)/shard_map/ppermute | solution.py:72
  195.7 6.8 %collective-permute-start.14 = (f32[4,64,64]{2,1,0:T(8,128)S(1)}, f32[4,64,64]{2,1,0:T(8,128)S(1)}, u32[]{:S(2)}, u32[]{:S(2)}) collective-permute-start(f32[4,64,64]{2,1,0:T(8,128)S(1)} %dynamic-slice_bitcast_fusion.3), channel_id=1, source_target_pairs={{0,4},{4,12},{12,20},{20,28},{28,24},{24,16},{16,8},{8,0},{1,5},{5... | collective-permute-start | bytes 196616 | tf_op jit(solution)/shard_map/ppermute | solution.py:72
  202.1 5.2 %collective-permute-start.22 = (f32[4,64,64]{2,1,0:T(8,128)S(1)}, f32[4,64,64]{2,1,0:T(8,128)S(1)}, u32[]{:S(2)}, u32[]{:S(2)}) collective-permute-start(f32[4,64,64]{2,1,0:T(8,128)S(1)} %bitcast_add_fusion.20), channel_id=1, source_target_pairs={{0,8},{4,0},{12,4},{20,12},{28,20},{24,28},{16,24},{8,16},{1,9},{5... | collective-permute-start | bytes 196616 | tf_op jit(solution)/shard_map/ppermute | solution.py:72
  202.6 6.1 %collective-permute-start.15 = (f32[4,64,64]{2,1,0:T(8,128)S(1)}, f32[4,64,64]{2,1,0:T(8,128)S(1)}, u32[]{:S(2)}, u32[]{:S(2)}) collective-permute-start(f32[4,64,64]{2,1,0:T(8,128)S(1)} %bitcast_add_fusion.27), channel_id=1, source_target_pairs={{0,4},{4,12},{12,20},{20,28},{28,24},{24,16},{16,8},{8,0},{1,5},{5... | collective-permute-start | bytes 196616 | tf_op jit(solution)/shard_map/ppermute | solution.py:72
  208.3 5.0 %collective-permute-start.23 = (f32[4,64,64]{2,1,0:T(8,128)S(1)}, f32[4,64,64]{2,1,0:T(8,128)S(1)}, u32[]{:S(2)}, u32[]{:S(2)}) collective-permute-start(f32[4,64,64]{2,1,0:T(8,128)S(1)} %bitcast_add_fusion.19), channel_id=1, source_target_pairs={{0,8},{4,0},{12,4},{20,12},{28,20},{24,28},{16,24},{8,16},{1,9},{5... | collective-permute-start | bytes 196616 | tf_op jit(solution)/shard_map/ppermute | solution.py:72
  208.7 5.9 %collective-permute-start.16 = (f32[4,64,64]{2,1,0:T(8,128)S(1)}, f32[4,64,64]{2,1,0:T(8,128)S(1)}, u32[]{:S(2)}, u32[]{:S(2)}) collective-permute-start(f32[4,64,64]{2,1,0:T(8,128)S(1)} %bitcast_add_fusion.26), channel_id=1, source_target_pairs={{0,4},{4,12},{12,20},{20,28},{28,24},{24,16},{16,8},{8,0},{1,5},{5... | collective-permute-start | bytes 196616 | tf_op jit(solution)/shard_map/ppermute | solution.py:72
  214.2 5.0 %collective-permute-start.24 = (f32[4,64,64]{2,1,0:T(8,128)S(1)}, f32[4,64,64]{2,1,0:T(8,128)S(1)}, u32[]{:S(2)}, u32[]{:S(2)}) collective-permute-start(f32[4,64,64]{2,1,0:T(8,128)S(1)} %bitcast_add_fusion.18), channel_id=1, source_target_pairs={{0,8},{4,0},{12,4},{20,12},{28,20},{24,28},{16,24},{8,16},{1,9},{5... | collective-permute-start | bytes 196616 | tf_op jit(solution)/shard_map/ppermute | solution.py:72
  214.7 5.9 %collective-permute-start.17 = (f32[4,64,64]{2,1,0:T(8,128)S(1)}, f32[4,64,64]{2,1,0:T(8,128)S(1)}, u32[]{:S(2)}, u32[]{:S(2)}) collective-permute-start(f32[4,64,64]{2,1,0:T(8,128)S(1)} %bitcast_add_fusion.25), channel_id=1, source_target_pairs={{0,4},{4,12},{12,20},{20,28},{28,24},{24,16},{16,8},{8,0},{1,5},{5... | collective-permute-start | bytes 196616 | tf_op jit(solution)/shard_map/ppermute | solution.py:72
  220.1 5.1 %collective-permute-start.25 = (f32[4,64,64]{2,1,0:T(8,128)S(1)}, f32[4,64,64]{2,1,0:T(8,128)S(1)}, u32[]{:S(2)}, u32[]{:S(2)}) collective-permute-start(f32[4,64,64]{2,1,0:T(8,128)S(1)} %bitcast_add_fusion.17), channel_id=1, source_target_pairs={{0,8},{4,0},{12,4},{20,12},{28,20},{24,28},{16,24},{8,16},{1,9},{5... | collective-permute-start | bytes 196616 | tf_op jit(solution)/shard_map/ppermute | solution.py:72
  220.6 12.0 %collective-permute-start.18 = (f32[4,64,64]{2,1,0:T(8,128)S(1)}, f32[4,64,64]{2,1,0:T(8,128)}, u32[]{:S(2)}, u32[]{:S(2)}) collective-permute-start(f32[4,64,64]{2,1,0:T(8,128)S(1)} %bitcast_add_fusion.24), channel_id=1, source_target_pairs={{0,4},{4,12},{12,20},{20,28},{28,24},{24,16},{16,8},{8,0},{1,5},{5... | collective-permute-start | bytes 196616 | tf_op jit(solution)/shard_map/ppermute | solution.py:72
  226.1 14.3 %collective-permute-start.26 = (f32[4,64,64]{2,1,0:T(8,128)S(1)}, f32[4,64,64]{2,1,0:T(8,128)S(1)}, u32[]{:S(2)}, u32[]{:S(2)}) collective-permute-start(f32[4,64,64]{2,1,0:T(8,128)S(1)} %bitcast_add_fusion.16), channel_id=1, source_target_pairs={{0,8},{4,0},{12,4},{20,12},{28,20},{24,28},{16,24},{8,16},{1,9},{5... | collective-permute-start | bytes 196616 | tf_op jit(solution)/shard_map/ppermute | solution.py:72
  228.4 1.3 copy-start.2
  230.4 42.3 %copy-start.5 = (f32[8,16,16,256]{3,1,0,2:T(8,128)}, f32[8,16,16,256]{3,1,0,2:T(8,128)S(1)}, u32[]{:S(2)}) copy-start(f32[8,16,16,256]{3,1,0,2:T(8,128)S(1)} %get-tuple-element.4) | copy-start | bytes 6291460
  230.4 43.4 %copy-start.4 = (f32[8,16,16,256]{3,1,0,2:T(8,128)}, f32[8,16,16,256]{3,1,0,2:T(8,128)S(1)}, u32[]{:S(2)}) copy-start(f32[8,16,16,256]{3,1,0,2:T(8,128)S(1)} %get-tuple-element.3) | copy-start | bytes 6291460
  230.5 7.2 %collective-permute-start.7 = (f32[16,16,256]{2,0,1:T(8,128)S(1)}, f32[16,16,256]{2,0,1:T(8,128)S(1)}, u32[]{:S(2)}, u32[]{:S(2)}) collective-permute-start(f32[16,16,256]{2,0,1:T(8,128)S(1)} %dynamic-slice_bitcast_fusion), channel_id=1, source_target_pairs={{0,8},{4,0},{12,4},{20,12},{28,20},{24,28},{16,24},{8,16},{1,9},{5... | collective-permute-start | bytes 786440 | tf_op jit(solution)/shard_map/ppermute | solution.py:72
  232.2 8.2 %collective-permute-start = (f32[16,16,256]{2,0,1:T(8,128)S(1)}, f32[16,16,256]{2,0,1:T(8,128)S(1)}, u32[]{:S(2)}, u32[]{:S(2)}) collective-permute-start(f32[16,16,256]{2,0,1:T(8,128)S(1)} %dynamic-slice_bitcast_fusion.1), channel_id=1, source_target_pairs={{0,4},{4,12},{12,20},{20,28},{28,24},{24,16},{16,8},{8,0},{1,5},{5... | collective-permute-start | bytes 786440 | tf_op jit(solution)/shard_map/ppermute | solution.py:72
  233.5 15.9 %collective-permute-start.19 = (f32[4,64,64]{2,1,0:T(8,128)S(1)}, f32[4,64,64]{2,1,0:T(8,128)S(1)}, u32[]{:S(2)}, u32[]{:S(2)}) collective-permute-start(f32[4,64,64]{2,1,0:T(8,128)S(1)} %bitcast_add_fusion.23), channel_id=1, source_target_pairs={{0,4},{4,12},{12,20},{20,28},{28,24},{24,16},{16,8},{8,0},{1,5},{5... | collective-permute-start | bytes 196616 | tf_op jit(solution)/shard_map/ppermute | solution.py:72
  237.7 9.0 %collective-permute-start.8 = (f32[16,16,256]{2,0,1:T(8,128)S(1)}, f32[16,16,256]{2,0,1:T(8,128)S(1)}, u32[]{:S(2)}, u32[]{:S(2)}) collective-permute-start(f32[16,16,256]{2,0,1:T(8,128)S(1)} %bitcast_add_fusion.6), channel_id=1, source_target_pairs={{0,8},{4,0},{12,4},{20,12},{28,20},{24,28},{16,24},{8,16},{1,9},{5... | collective-permute-start | bytes 786440 | tf_op jit(solution)/shard_map/ppermute | solution.py:72
  240.4 8.9 %collective-permute-start.1 = (f32[16,16,256]{2,0,1:T(8,128)S(1)}, f32[16,16,256]{2,0,1:T(8,128)S(1)}, u32[]{:S(2)}, u32[]{:S(2)}) collective-permute-start(f32[16,16,256]{2,0,1:T(8,128)S(1)} %bitcast_add_fusion.13), channel_id=1, source_target_pairs={{0,4},{4,12},{12,20},{20,28},{28,24},{24,16},{16,8},{8,0},{1,5},{5... | collective-permute-start | bytes 786440 | tf_op jit(solution)/shard_map/ppermute | solution.py:72
  241.4 17.0 %collective-permute-start.27 = (f32[4,64,64]{2,1,0:T(8,128)S(1)}, f32[4,64,64]{2,1,0:T(8,128)S(1)}, u32[]{:S(2)}, u32[]{:S(2)}) collective-permute-start(f32[4,64,64]{2,1,0:T(8,128)S(1)} %bitcast_add_fusion.15), channel_id=1, source_target_pairs={{0,8},{4,0},{12,4},{20,12},{28,20},{24,28},{16,24},{8,16},{1,9},{5... | collective-permute-start | bytes 196616 | tf_op jit(solution)/shard_map/ppermute | solution.py:72
  246.8 9.0 %collective-permute-start.9 = (f32[16,16,256]{2,0,1:T(8,128)S(1)}, f32[16,16,256]{2,0,1:T(8,128)S(1)}, u32[]{:S(2)}, u32[]{:S(2)}) collective-permute-start(f32[16,16,256]{2,0,1:T(8,128)S(1)} %bitcast_add_fusion.5), channel_id=1, source_target_pairs={{0,8},{4,0},{12,4},{20,12},{28,20},{24,28},{16,24},{8,16},{1,9},{5... | collective-permute-start | bytes 786440 | tf_op jit(solution)/shard_map/ppermute | solution.py:72
  249.3 9.0 %collective-permute-start.2 = (f32[16,16,256]{2,0,1:T(8,128)S(1)}, f32[16,16,256]{2,0,1:T(8,128)S(1)}, u32[]{:S(2)}, u32[]{:S(2)}) collective-permute-start(f32[16,16,256]{2,0,1:T(8,128)S(1)} %bitcast_add_fusion.12), channel_id=1, source_target_pairs={{0,4},{4,12},{12,20},{20,28},{28,24},{24,16},{16,8},{8,0},{1,5},{5... | collective-permute-start | bytes 786440 | tf_op jit(solution)/shard_map/ppermute | solution.py:72
  249.4 17.5 %collective-permute-start.20 = (f32[4,64,64]{2,1,0:T(8,128)S(1)}, f32[4,64,64]{2,1,0:T(8,128)S(1)}, u32[]{:S(2)}, u32[]{:S(2)}) collective-permute-start(f32[4,64,64]{2,1,0:T(8,128)S(1)} %bitcast_add_fusion.22), channel_id=1, source_target_pairs={{0,4},{4,12},{12,20},{20,28},{28,24},{24,16},{16,8},{8,0},{1,5},{5... | collective-permute-start | bytes 196616 | tf_op jit(solution)/shard_map/ppermute | solution.py:72
  255.8 8.9 %collective-permute-start.10 = (f32[16,16,256]{2,0,1:T(8,128)S(1)}, f32[16,16,256]{2,0,1:T(8,128)S(1)}, u32[]{:S(2)}, u32[]{:S(2)}) collective-permute-start(f32[16,16,256]{2,0,1:T(8,128)S(1)} %bitcast_add_fusion.4), channel_id=1, source_target_pairs={{0,8},{4,0},{12,4},{20,12},{28,20},{24,28},{16,24},{8,16},{1,9},{5... | collective-permute-start | bytes 786440 | tf_op jit(solution)/shard_map/ppermute | solution.py:72
  258.3 8.1 %collective-permute-start.3 = (f32[16,16,256]{2,0,1:T(8,128)S(1)}, f32[16,16,256]{2,0,1:T(8,128)S(1)}, u32[]{:S(2)}, u32[]{:S(2)}) collective-permute-start(f32[16,16,256]{2,0,1:T(8,128)S(1)} %bitcast_add_fusion.11), channel_id=1, source_target_pairs={{0,4},{4,12},{12,20},{20,28},{28,24},{24,16},{16,8},{8,0},{1,5},{5... | collective-permute-start | bytes 786440 | tf_op jit(solution)/shard_map/ppermute | solution.py:72
  264.7 8.0 %collective-permute-start.11 = (f32[16,16,256]{2,0,1:T(8,128)S(1)}, f32[16,16,256]{2,0,1:T(8,128)S(1)}, u32[]{:S(2)}, u32[]{:S(2)}) collective-permute-start(f32[16,16,256]{2,0,1:T(8,128)S(1)} %bitcast_add_fusion.3), channel_id=1, source_target_pairs={{0,8},{4,0},{12,4},{20,12},{28,20},{24,28},{16,24},{8,16},{1,9},{5... | collective-permute-start | bytes 786440 | tf_op jit(solution)/shard_map/ppermute | solution.py:72
  266.5 7.3 %collective-permute-start.4 = (f32[16,16,256]{2,0,1:T(8,128)S(1)}, f32[16,16,256]{2,0,1:T(8,128)S(1)}, u32[]{:S(2)}, u32[]{:S(2)}) collective-permute-start(f32[16,16,256]{2,0,1:T(8,128)S(1)} %bitcast_add_fusion.10), channel_id=1, source_target_pairs={{0,4},{4,12},{12,20},{20,28},{28,24},{24,16},{16,8},{8,0},{1,5},{5... | collective-permute-start | bytes 786440 | tf_op jit(solution)/shard_map/ppermute | solution.py:72
  272.7 8.0 %collective-permute-start.12 = (f32[16,16,256]{2,0,1:T(8,128)S(1)}, f32[16,16,256]{2,0,1:T(8,128)S(1)}, u32[]{:S(2)}, u32[]{:S(2)}) collective-permute-start(f32[16,16,256]{2,0,1:T(8,128)S(1)} %bitcast_add_fusion.2), channel_id=1, source_target_pairs={{0,8},{4,0},{12,4},{20,12},{28,20},{24,28},{16,24},{8,16},{1,9},{5... | collective-permute-start | bytes 786440 | tf_op jit(solution)/shard_map/ppermute | solution.py:72
  273.8 8.3 %collective-permute-start.5 = (f32[16,16,256]{2,0,1:T(8,128)S(1)}, f32[16,16,256]{2,0,1:T(8,128)S(1)}, u32[]{:S(2)}, u32[]{:S(2)}) collective-permute-start(f32[16,16,256]{2,0,1:T(8,128)S(1)} %bitcast_add_fusion.9), channel_id=1, source_target_pairs={{0,4},{4,12},{12,20},{20,28},{28,24},{24,16},{16,8},{8,0},{1,5},{5... | collective-permute-start | bytes 786440 | tf_op jit(solution)/shard_map/ppermute | solution.py:72
  281.7 8.0 %collective-permute-start.13 = (f32[16,16,256]{2,0,1:T(8,128)S(1)}, f32[16,16,256]{2,0,1:T(8,128)S(1)}, u32[]{:S(2)}, u32[]{:S(2)}) collective-permute-start(f32[16,16,256]{2,0,1:T(8,128)S(1)} %bitcast_add_fusion.1), channel_id=1, source_target_pairs={{0,8},{4,0},{12,4},{20,12},{28,20},{24,28},{16,24},{8,16},{1,9},{5... | collective-permute-start | bytes 786440 | tf_op jit(solution)/shard_map/ppermute | solution.py:72
  283.1 7.7 %collective-permute-start.6 = (f32[16,16,256]{2,0,1:T(8,128)S(1)}, f32[16,16,256]{2,0,1:T(8,128)S(1)}, u32[]{:S(2)}, u32[]{:S(2)}) collective-permute-start(f32[16,16,256]{2,0,1:T(8,128)S(1)} %bitcast_add_fusion.8), channel_id=1, source_target_pairs={{0,4},{4,12},{12,20},{20,28},{28,24},{24,16},{16,8},{8,0},{1,5},{5... | collective-permute-start | bytes 786440 | tf_op jit(solution)/shard_map/ppermute | solution.py:72
Sparse Core Ops, SparseCore 0:
  13.1 88.9 all-gather.2
where the time goes:
time: 301 us; the launch traced here: 299 us
  waiting for transfers between devices  122 us (41%)
  between operations  55.1 us (18%)
  starting transfers between devices  46.6 us (15%)
  local copies, waits for them, and re-layouts  44.2 us (15%)
  other arithmetic  16.3 us (5%)
  matrix products  14.8 us (5%)
    all_gather x1, waiting for transfers between devices, body(): packed = lax.all_gather(packed, 'dp', axis=0, tiled=True)  80.6 us
    ppermute x28, waiting for transfers between devices, ring_reduce_scatter(): acc = lax.ppermute(acc, 'dp', pairs)  41.8 us
    ppermute x28, starting transfers between devices, ring_reduce_scatter(): acc = lax.ppermute(acc, 'dp', pairs)  32.9 us
    add x28, other arithmetic, ring_reduce_scatter(): acc = mine if acc is None else acc + mine  11.8 us
    unnamed x20, local copies, waits for them, and re-layouts  10.3 us
  transfers between devices with their start and end apart: 32, of which 13 were waited for; matrix products, arithmetic and copies ran while one was open for 15% of the time, Pallas kernels for 0%

commit v1 on v0

--- a/solution.py
+++ b/solution.py
@@ -86,7 +86,12 @@
     rows_r = r_mix.shape[1]
     r_flat = r_mix.reshape(1, -1)
     packed = jnp.concatenate([r_flat, l_mix.reshape(1, -1)], axis=1)
-    packed = lax.all_gather(packed, "dp", axis=0, tiled=True)
+    ring_ = [packed]
+    for hop in range(7):
+        ring_.append(lax.ppermute(ring_[-1], "dp", [(dev, (dev + 1) % 8) for dev in range(8)]))
+    packed = jnp.roll(
+        jnp.concatenate(ring_[::-1], axis=0), (lax.axis_index("dp") + 1) * ring_[0].shape[0], axis=0
+    )
     r_size = r_flat.shape[1]
     r_whole = packed[:, :r_size].reshape(n_dp, local_blocks, rows_r, WIDTH)
     r_whole = jnp.transpose(r_whole, (1, 0, 2, 3)).reshape(local_blocks, n_dp * rows_r, WIDTH)

time: 301 us -> 342 us (1.14)
  local copies, waits for them, and re-layouts: 44.2 us -> 72.2 us
  waiting for transfers between devices: 122 us -> 150 us
  between operations: 55.1 us -> 41.4 us
  other arithmetic: 16.3 us -> 12.7 us
    ppermute x0 -> x7, waiting for transfers between devices: none -> 107 us  [body(): lax.ppermute(ring_[-1], 'dp', [(dev, (dev + 1) % 8) for dev in range(8)])]
    all_gather x1 -> x0, waiting for transfers between devices: 80.6 us -> none  [body(): packed = lax.all_gather(packed, 'dp', axis=0, tiled=True)]
    concatenate x0 -> x2, local copies, waits for them, and re-layouts: none -> 28.1 us  [the longest x1 28 us: body(): jnp.roll(jnp.concatenate(ring_[::-1], axis=0), (lax.axis_index('dp') + 1)...]
    unnamed x1 -> x0, other arithmetic: 3.62 us -> none
    unnamed x20 -> x26, local copies, waits for them, and re-layouts: 10.3 us -> 7.01 us
  transfers between devices with their start and end apart: 32 -> 38, of which waited for: 13 -> 19; matrix products, arithmetic and copies ran while one was open for 15% -> 21% of each run, Pallas kernels for 0% -> 0%
where the time goes in v1:
time: 342 us; the launch traced here: 338 us
  waiting for transfers between devices  150 us (44%)
  local copies, waits for them, and re-layouts  72.2 us (21%)
  starting transfers between devices  47.1 us (14%)
  between operations  41.4 us (12%)
  matrix products  14.9 us (4%)
  other arithmetic  12.7 us (4%)
    ppermute x7, waiting for transfers between devices, body(): lax.ppermute(ring_[-1], 'dp', [(dev, (dev + 1) % 8) for dev in range(8)])  107 us
    ppermute x28, waiting for transfers between devices, ring_reduce_scatter(): acc = lax.ppermute(acc, 'dp', pairs)  42 us
    ppermute x28, starting transfers between devices, ring_reduce_scatter(): acc = lax.ppermute(acc, 'dp', pairs)  30.4 us
    concatenate x1, local copies, waits for them, and re-layouts, body(): jnp.roll(jnp.concatenate(ring_[::-1], axis=0), (lax.axis_index('dp') + 1)...  28 us
    add x28, other arithmetic, ring_reduce_scatter(): acc = mine if acc is None else acc + mine  11.8 us
    unnamed x26, local copies, waits for them, and re-layouts  7.01 us
  transfers between devices with their start and end apart: 38, of which 19 were waited for; matrix products, arithmetic and copies ran while one was open for 21% of the time, Pallas kernels for 0%

profile of v1, /device:TPU:0, one launch (start us, length us, event | category | flops | bytes accessed | tf_op | source)
XLA Modules:
  0.0 337.8 jit_solution(312702770908409246)
XLA Ops:
  0.6 1.1 copy.49
  1.7 1.0 reshape.111
  3.5 3.0 collective-permute-start
  6.5 17.8 %collective-permute-done = bf16[1,163840]{1,0:T(2,128)(2,1)S(1)} collective-permute-done((bf16[1,163840]{1,0:T(2,128)(2,1)S(1)}, bf16[1,163840]{1,0:T(2,128)(2,1)S(1)}, u32[]{:S(2)}, u32[]{:S(2)}) %collective-permute-start) | collective-permute-done | bytes 327712 | tf_op jit(solution)/shard_map/ppermute | solution.py:91
  24.3 18.6 %collective-permute-done.1 = bf16[1,163840]{1,0:T(2,128)(2,1)S(1)} collective-permute-done((bf16[1,163840]{1,0:T(2,128)(2,1)S(1)}, bf16[1,163840]{1,0:T(2,128)(2,1)S(1)}, u32[]{:S(2)}, u32[]{:S(2)}) %collective-permute-start.1) | collective-permute-done | bytes 327712 | tf_op jit(solution)/shard_map/ppermute | solution.py:91
  43.7 17.7 %collective-permute-done.2 = bf16[1,163840]{1,0:T(2,128)(2,1)S(1)} collective-permute-done((bf16[1,163840]{1,0:T(2,128)(2,1)S(1)}, bf16[1,163840]{1,0:T(2,128)(2,1)S(1)}, u32[]{:S(2)}, u32[]{:S(2)}) %collective-permute-start.2) | collective-permute-done | bytes 327712 | tf_op jit(solution)/shard_map/ppermute | solution.py:91
  62.4 16.8 %collective-permute-done.3 = bf16[1,163840]{1,0:T(2,128)(2,1)S(1)} collective-permute-done((bf16[1,163840]{1,0:T(2,128)(2,1)S(1)}, bf16[1,163840]{1,0:T(2,128)(2,1)S(1)}, u32[]{:S(2)}, u32[]{:S(2)}) %collective-permute-start.3) | collective-permute-done | bytes 327712 | tf_op jit(solution)/shard_map/ppermute | solution.py:91
  80.0 15.8 %collective-permute-done.4 = bf16[1,163840]{1,0:T(2,128)(2,1)S(1)} collective-permute-done((bf16[1,163840]{1,0:T(2,128)(2,1)S(1)}, bf16[1,163840]{1,0:T(2,128)(2,1)S(1)}, u32[]{:S(2)}, u32[]{:S(2)}) %collective-permute-start.4) | collective-permute-done | bytes 327712 | tf_op jit(solution)/shard_map/ppermute | solution.py:91
  96.7 15.0 %collective-permute-done.5 = bf16[1,163840]{1,0:T(2,128)(2,1)} collective-permute-done((bf16[1,163840]{1,0:T(2,128)(2,1)S(1)}, bf16[1,163840]{1,0:T(2,128)(2,1)}, u32[]{:S(2)}, u32[]{:S(2)}) %collective-permute-start.5) | collective-permute-done | bytes 327712 | tf_op jit(solution)/shard_map/ppermute | solution.py:91
  111.8 4.1 %copy.37 = bf16[16,256,256]{2,0,1:T(8,128)(2,1)} copy(bf16[16,256,256]{2,1,0:T(8,128)(2,1)} %bitcast.176) | data formatting | bytes 4194304 | tf_op jit(solution)/shard_map/reshape | solution.py:83
  115.8 4.5 %all-to-all-start = ((bf16[16,256,256]{2,0,1:T(8,128)(2,1)}), bf16[16,256,256]{2,0,1:T(8,128)(2,1)}, u32[]{:S(2)}, u32[]{:S(2)}) async-start(bf16[16,256,256]{2,0,1:T(8,128)(2,1)} %copy.37), calls=%async_computation | async-start | bytes 4194304 | tf_op jit(solution)/shard_map/all_to_all | solution.py:84
  120.3 5.7 %collective-permute-done.6 = bf16[1,163840]{1,0:T(2,128)(2,1)} collective-permute-done((bf16[1,163840]{1,0:T(2,128)(2,1)}, bf16[1,163840]{1,0:T(2,128)(2,1)}, u32[]{:S(2)}, u32[]{:S(2)}) %collective-permute-start.6) | collective-permute-done | bytes 327712 | tf_op jit(solution)/shard_map/ppermute | solution.py:91
  126.1 28.0 %concatenate.16 = bf16[16,163840]{1,0:T(8,128)(2,1)} concatenate(bf16[1,163840]{1,0:T(2,128)(2,1)} %collective-permute-done.6, bf16[1,163840]{1,0:T(2,128)(2,1)} %collective-permute-done.5, bf16[1,163840]{1,0:T(2,128)(2,1)} %copy-done.9, bf16[1,163840]{1,0:T(2,128)(2,1)} %copy-done.8, bf16[1,163840]{1,0:T(2,128)(2,1)} %copy-done.7, bf16[1,163840]{1,0:T(2,128)(2,1)} %copy-done.6, ...), dimensions={0} | concatenate | bytes 10485760 | tf_op jit(solution)/shard_map/jit(_roll_dynamic)/concatenate | solution.py:92
  154.1 2.8 constant_dynamic-slice_fusion
  158.8 2.5 copy.40
  161.3 4.8 %all-to-all-start.1 = ((bf16[16,256,256]{2,0,1:T(8,128)(2,1)}), bf16[16,256,256]{2,0,1:T(8,128)(2,1)}, u32[]{:S(2)}, u32[]{:S(2)}) async-start(bf16[16,256,256]{2,0,1:T(8,128)(2,1)} %copy.40), calls=%async_computation.1 | async-start | bytes 4194304 | tf_op jit(solution)/shard_map/all_to_all | solution.py:103
  207.8 4.2 %copy.38 = f32[16,4,64,256]{3,0,1,2:T(8,128)} copy(bf16[16,4,64,256]{3,0,2,1:T(8,128)(2,1)} %bitcast.91) | data formatting | bytes 6291456 | tf_op jit(solution)/shard_map/convert_element_type | solution.py:18
  212.0 1.5 dynamic-slice.1
  213.5 2.1 reshape.115
  215.6 1.5 copy.36
  217.1 2.0 copy.41
  220.0 5.1 %fusion.6 = bf16[64,64,256]{2,0,1:T(8,128)(2,1)S(1)} fusion(f32[16,4,64,256]{3,0,1,2:T(8,128)S(1)} %copy-done.5, bf16[64,64,256]{2,0,1:T(8,128)(2,1)S(1)} %bitcast.172, bf16[64,64,64]{2,1,0:T(8,128)(2,1)S(1)} %bitcast.178), kind=kOutput, calls=%fused_computation.8 | convolution fusion | flops 155189248 | bytes 8912896 | tf_op jit(solution)/shard_map/bst,bsc->cst/dot_general | solution.py:104
  225.0 2.1 multiply_bitcast_fusion
  227.1 1.3 convolution_convert_fusion
  228.4 2.5 copy.44
  230.9 3.8 %copy.46 = f32[64,64,64]{2,1,0:T(8,128)} copy(f32[64,64,64]{0,2,1:T(8,128)} %multiply_bitcast_fusion) | data formatting | bytes 2097152 | tf_op jit(solution)/shard_map/mul | solution.py:110
  234.7 2.7 fusion.13
  237.4 4.4 %all-to-all-start.2 = ((bf16[64,64,256]{2,0,1:T(8,128)(2,1)}), bf16[64,64,256]{2,0,1:T(8,128)(2,1)}, u32[]{:S(2)}, u32[]{:S(2)}) async-start(bf16[64,64,256]{2,0,1:T(8,128)(2,1)} %copy.44), calls=%async_computation.2 | async-start | bytes 4194304 | tf_op jit(solution)/shard_map/all_to_all | solution.py:113
  242.9 2.1 collective-permute-start.21
  244.9 3.8 %collective-permute-done.28 = f32[4,64,64]{2,1,0:T(8,128)S(1)} collective-permute-done((f32[4,64,64]{2,1,0:T(8,128)S(1)}, f32[4,64,64]{2,1,0:T(8,128)S(1)}, u32[]{:S(2)}, u32[]{:S(2)}) %collective-permute-start.28) | collective-permute-done | bytes 65568 | tf_op jit(solution)/shard_map/ppermute | solution.py:72
  248.7 0.9 bitcast_add_fusion.20
  250.0 1.8 collective-permute-start.22
  251.8 3.1 collective-permute-done.29
  254.9 0.9 bitcast_add_fusion.19
  256.4 1.6 collective-permute-start.23
  257.9 2.9 collective-permute-done.30
  262.3 1.6 collective-permute-start.24
  263.9 2.9 collective-permute-done.31
  266.7 0.9 bitcast_add_fusion.17
  268.2 1.6 collective-permute-start.25
  269.8 2.9 collective-permute-done.32
  274.4 1.8 copy.45
  278.6 1.8 collective-permute-start.7
  281.3 1.6 collective-permute-start.26
  283.0 3.0 collective-permute-done.14
  286.7 2.1 collective-permute-start.8
  289.8 5.9 %collective-permute-done.15 = f32[16,16,256]{2,0,1:T(8,128)S(1)} collective-permute-done((f32[16,16,256]{2,0,1:T(8,128)S(1)}, f32[16,16,256]{2,0,1:T(8,128)S(1)}, u32[]{:S(2)}, u32[]{:S(2)}) %collective-permute-start.15) | collective-permute-done | bytes 262176 | tf_op jit(solution)/shard_map/ppermute | solution.py:72
  295.9 2.1 collective-permute-start.9
  298.0 2.2 collective-permute-start.27
  300.1 4.2 %collective-permute-done.16 = f32[16,16,256]{2,0,1:T(8,128)S(1)} collective-permute-done((f32[16,16,256]{2,0,1:T(8,128)S(1)}, f32[16,16,256]{2,0,1:T(8,128)S(1)}, u32[]{:S(2)}, u32[]{:S(2)}) %collective-permute-start.16) | collective-permute-done | bytes 262176 | tf_op jit(solution)/shard_map/ppermute | solution.py:72
  304.8 1.8 collective-permute-start.10
  306.6 0.9 bitcast_add_fusion.14
  307.5 4.7 %collective-permute-done.17 = f32[16,16,256]{2,0,1:T(8,128)S(1)} collective-permute-done((f32[16,16,256]{2,0,1:T(8,128)S(1)}, f32[16,16,256]{2,0,1:T(8,128)S(1)}, u32[]{:S(2)}, u32[]{:S(2)}) %collective-permute-start.17) | collective-permute-done | bytes 262176 | tf_op jit(solution)/shard_map/ppermute | solution.py:72
  312.9 1.5 collective-permute-start.11
  314.4 4.7 %collective-permute-done.18 = f32[16,16,256]{2,0,1:T(8,128)S(1)} collective-permute-done((f32[16,16,256]{2,0,1:T(8,128)S(1)}, f32[16,16,256]{2,0,1:T(8,128)S(1)}, u32[]{:S(2)}, u32[]{:S(2)}) %collective-permute-start.18) | collective-permute-done | bytes 262176 | tf_op jit(solution)/shard_map/ppermute | solution.py:72
  319.1 1.0 collective-permute-start.19
  320.2 1.1 collective-permute-start.12
  322.2 3.7 %collective-permute-done.19 = f32[16,16,256]{2,0,1:T(8,128)S(1)} collective-permute-done((f32[16,16,256]{2,0,1:T(8,128)S(1)}, f32[16,16,256]{2,0,1:T(8,128)S(1)}, u32[]{:S(2)}, u32[]{:S(2)}) %collective-permute-start.19) | collective-permute-done | bytes 262176 | tf_op jit(solution)/shard_map/ppermute | solution.py:72
  326.0 1.0 bitcast_add_fusion.1
  327.0 1.4 collective-permute-start.20
  328.4 1.0 bitcast_add_fusion.8
  330.1 4.9 %add_convert_fusion = bf16[16,256,256]{2,1,0:T(8,128)(2,1)} fusion(bf16[16,256,256]{2,1,0:T(8,128)(2,1)} %bitcast.177, bf16[16,256,256]{2,1,0:T(8,128)(2,1)} %bitcast.168, bf16[256,16,256]{2,0,1:T(8,128)(2,1)} %bitcast.170), kind=kOutput, calls=%fused_computation.14 | convolution fusion | flops 540016640 | bytes 8388608 | tf_op jit(solution)/shard_map/obt,bio->bit/dot_general | solution.py:114
  335.0 1.0 bitcast_add_fusion
  336.0 1.0 bitcast_add_fusion.7
  (99 shorter events, 22.7 us)
Async XLA Ops:
  0.6 156.8 %copy-start = (bf16[4096,256]{1,0:T(8,128)(2,1)S(1)}, bf16[4096,256]{1,0:T(8,128)(2,1)}, u32[]{:S(2)}) copy-start(bf16[4096,256]{1,0:T(8,128)(2,1)} %param.8) | copy-start | bytes 6291460
  3.5 20.8 %collective-permute-start = (bf16[1,163840]{1,0:T(2,128)(2,1)S(1)}, bf16[1,163840]{1,0:T(2,128)(2,1)S(1)}, u32[]{:S(2)}, u32[]{:S(2)}) collective-permute-start(bf16[1,163840]{1,0:T(2,128)(2,1)S(1)} %constant_dynamic-update-slice_fusion), channel_id=1, source_target_pairs={{0,4},{4,8},{8,12},{12,16},{16,20},{20,24},{24,28},{28,0},{1,5},{5... | collective-permute-start | bytes 983048 | tf_op jit(solution)/shard_map/ppermute | solution.py:91
  24.3 18.6 %collective-permute-start.1 = (bf16[1,163840]{1,0:T(2,128)(2,1)S(1)}, bf16[1,163840]{1,0:T(2,128)(2,1)S(1)}, u32[]{:S(2)}, u32[]{:S(2)}) collective-permute-start(bf16[1,163840]{1,0:T(2,128)(2,1)S(1)} %collective-permute-done), channel_id=1, source_target_pairs={{0,4},{4,8},{8,12},{12,16},{16,20},{20,24},{24,28},{28,0},{1,5},{5... | collective-permute-start | bytes 983048 | tf_op jit(solution)/shard_map/ppermute | solution.py:91
  42.9 0.8 copy-start.6
  43.7 17.7 %collective-permute-start.2 = (bf16[1,163840]{1,0:T(2,128)(2,1)S(1)}, bf16[1,163840]{1,0:T(2,128)(2,1)S(1)}, u32[]{:S(2)}, u32[]{:S(2)}) collective-permute-start(bf16[1,163840]{1,0:T(2,128)(2,1)S(1)} %collective-permute-done.1), channel_id=1, source_target_pairs={{0,4},{4,8},{8,12},{12,16},{16,20},{20,24},{24,28},{28,0},{1,5},{5... | collective-permute-start | bytes 983048 | tf_op jit(solution)/shard_map/ppermute | solution.py:91
  61.4 0.9 copy-start.7
  62.4 16.8 %collective-permute-start.3 = (bf16[1,163840]{1,0:T(2,128)(2,1)S(1)}, bf16[1,163840]{1,0:T(2,128)(2,1)S(1)}, u32[]{:S(2)}, u32[]{:S(2)}) collective-permute-start(bf16[1,163840]{1,0:T(2,128)(2,1)S(1)} %collective-permute-done.2), channel_id=1, source_target_pairs={{0,4},{4,8},{8,12},{12,16},{16,20},{20,24},{24,28},{28,0},{1,5},{5... | collective-permute-start | bytes 983048 | tf_op jit(solution)/shard_map/ppermute | solution.py:91
  79.1 0.9 copy-start.8
  80.0 15.9 %collective-permute-start.4 = (bf16[1,163840]{1,0:T(2,128)(2,1)S(1)}, bf16[1,163840]{1,0:T(2,128)(2,1)S(1)}, u32[]{:S(2)}, u32[]{:S(2)}) collective-permute-start(bf16[1,163840]{1,0:T(2,128)(2,1)S(1)} %collective-permute-done.3), channel_id=1, source_target_pairs={{0,4},{4,8},{8,12},{12,16},{16,20},{20,24},{24,28},{28,0},{1,5},{5... | collective-permute-start | bytes 983048 | tf_op jit(solution)/shard_map/ppermute | solution.py:91
  95.9 0.8 copy-start.9
  96.7 15.0 %collective-permute-start.5 = (bf16[1,163840]{1,0:T(2,128)(2,1)S(1)}, bf16[1,163840]{1,0:T(2,128)(2,1)}, u32[]{:S(2)}, u32[]{:S(2)}) collective-permute-start(bf16[1,163840]{1,0:T(2,128)(2,1)S(1)} %collective-permute-done.4), channel_id=1, source_target_pairs={{0,4},{4,8},{8,12},{12,16},{16,20},{20,24},{24,28},{28,0},{1,5},{5... | collective-permute-start | bytes 983048 | tf_op jit(solution)/shard_map/ppermute | solution.py:91
  111.8 14.3 %collective-permute-start.6 = (bf16[1,163840]{1,0:T(2,128)(2,1)}, bf16[1,163840]{1,0:T(2,128)(2,1)}, u32[]{:S(2)}, u32[]{:S(2)}) collective-permute-start(bf16[1,163840]{1,0:T(2,128)(2,1)} %collective-permute-done.5), channel_id=1, source_target_pairs={{0,4},{4,8},{8,12},{12,16},{16,20},{20,24},{24,28},{28,0},{1,5},{5... | collective-permute-start | bytes 983048 | tf_op jit(solution)/shard_map/ppermute | solution.py:91
  115.8 45.4 %all-to-all-start = ((bf16[16,256,256]{2,0,1:T(8,128)(2,1)}), bf16[16,256,256]{2,0,1:T(8,128)(2,1)}, u32[]{:S(2)}, u32[]{:S(2)}) async-start(bf16[16,256,256]{2,0,1:T(8,128)(2,1)} %copy.37), calls=%async_computation | async-start | bytes 4194304 | tf_op jit(solution)/shard_map/all_to_all | solution.py:84
  157.5 1.3 copy-start.1
  161.3 4.8 %copy-start.11 = (s32[8]{0:T(128)S(1)}, s32[8]{0:T(128)}, u32[]{:S(2)}) copy-start(s32[8]{0:T(128)} %constant.344.clone) | copy-start | bytes 100
  161.3 16.1 %copy-start.10 = (s32[8]{0:T(128)S(1)}, s32[8]{0:T(128)}, u32[]{:S(2)}) copy-start(s32[8]{0:T(128)} %constant.343.clone) | copy-start | bytes 100
  161.3 55.9 %all-to-all-start.1 = ((bf16[16,256,256]{2,0,1:T(8,128)(2,1)}), bf16[16,256,256]{2,0,1:T(8,128)(2,1)}, u32[]{:S(2)}, u32[]{:S(2)}) async-start(bf16[16,256,256]{2,0,1:T(8,128)(2,1)} %copy.40), calls=%async_computation.1 | async-start | bytes 4194304 | tf_op jit(solution)/shard_map/all_to_all | solution.py:103
  217.1 2.8 copy-start.5
  237.4 37.0 %all-to-all-start.2 = ((bf16[64,64,256]{2,0,1:T(8,128)(2,1)}), bf16[64,64,256]{2,0,1:T(8,128)(2,1)}, u32[]{:S(2)}, u32[]{:S(2)}) async-start(bf16[64,64,256]{2,0,1:T(8,128)(2,1)} %copy.44), calls=%async_computation.2 | async-start | bytes 4194304 | tf_op jit(solution)/shard_map/all_to_all | solution.py:113
  242.8 5.9 %collective-permute-start.28 = (f32[4,64,64]{2,1,0:T(8,128)S(1)}, f32[4,64,64]{2,1,0:T(8,128)S(1)}, u32[]{:S(2)}, u32[]{:S(2)}) collective-permute-start(f32[4,64,64]{2,1,0:T(8,128)S(1)} %dynamic-slice_bitcast_fusion.2), channel_id=1, source_target_pairs={{0,8},{4,0},{12,4},{20,12},{28,20},{24,28},{16,24},{8,16},{1,9},{5... | collective-permute-start | bytes 196616 | tf_op jit(solution)/shard_map/ppermute | solution.py:72
  242.9 7.1 %collective-permute-start.21 = (f32[4,64,64]{2,1,0:T(8,128)S(1)}, f32[4,64,64]{2,1,0:T(8,128)S(1)}, u32[]{:S(2)}, u32[]{:S(2)}) collective-permute-start(f32[4,64,64]{2,1,0:T(8,128)S(1)} %dynamic-slice_bitcast_fusion.3), channel_id=1, source_target_pairs={{0,4},{4,12},{12,20},{20,28},{28,24},{24,16},{16,8},{8,0},{1,5},{5... | collective-permute-start | bytes 196616 | tf_op jit(solution)/shard_map/ppermute | solution.py:72
  249.6 5.2 %collective-permute-start.29 = (f32[4,64,64]{2,1,0:T(8,128)S(1)}, f32[4,64,64]{2,1,0:T(8,128)S(1)}, u32[]{:S(2)}, u32[]{:S(2)}) collective-permute-start(f32[4,64,64]{2,1,0:T(8,128)S(1)} %bitcast_add_fusion.20), channel_id=1, source_target_pairs={{0,8},{4,0},{12,4},{20,12},{28,20},{24,28},{16,24},{8,16},{1,9},{5... | collective-permute-start | bytes 196616 | tf_op jit(solution)/shard_map/ppermute | solution.py:72
  250.0 6.3 %collective-permute-start.22 = (f32[4,64,64]{2,1,0:T(8,128)S(1)}, f32[4,64,64]{2,1,0:T(8,128)S(1)}, u32[]{:S(2)}, u32[]{:S(2)}) collective-permute-start(f32[4,64,64]{2,1,0:T(8,128)S(1)} %bitcast_add_fusion.27), channel_id=1, source_target_pairs={{0,4},{4,12},{12,20},{20,28},{28,24},{24,16},{16,8},{8,0},{1,5},{5... | collective-permute-start | bytes 196616 | tf_op jit(solution)/shard_map/ppermute | solution.py:72
  255.8 5.0 %collective-permute-start.30 = (f32[4,64,64]{2,1,0:T(8,128)S(1)}, f32[4,64,64]{2,1,0:T(8,128)S(1)}, u32[]{:S(2)}, u32[]{:S(2)}) collective-permute-start(f32[4,64,64]{2,1,0:T(8,128)S(1)} %bitcast_add_fusion.19), channel_id=1, source_target_pairs={{0,8},{4,0},{12,4},{20,12},{28,20},{24,28},{16,24},{8,16},{1,9},{5... | collective-permute-start | bytes 196616 | tf_op jit(solution)/shard_map/ppermute | solution.py:72
  256.4 5.9 %collective-permute-start.23 = (f32[4,64,64]{2,1,0:T(8,128)S(1)}, f32[4,64,64]{2,1,0:T(8,128)S(1)}, u32[]{:S(2)}, u32[]{:S(2)}) collective-permute-start(f32[4,64,64]{2,1,0:T(8,128)S(1)} %bitcast_add_fusion.26), channel_id=1, source_target_pairs={{0,4},{4,12},{12,20},{20,28},{28,24},{24,16},{16,8},{8,0},{1,5},{5... | collective-permute-start | bytes 196616 | tf_op jit(solution)/shard_map/ppermute | solution.py:72
  261.7 5.0 %collective-permute-start.31 = (f32[4,64,64]{2,1,0:T(8,128)S(1)}, f32[4,64,64]{2,1,0:T(8,128)S(1)}, u32[]{:S(2)}, u32[]{:S(2)}) collective-permute-start(f32[4,64,64]{2,1,0:T(8,128)S(1)} %bitcast_add_fusion.18), channel_id=1, source_target_pairs={{0,8},{4,0},{12,4},{20,12},{28,20},{24,28},{16,24},{8,16},{1,9},{5... | collective-permute-start | bytes 196616 | tf_op jit(solution)/shard_map/ppermute | solution.py:72
  262.3 5.9 %collective-permute-start.24 = (f32[4,64,64]{2,1,0:T(8,128)S(1)}, f32[4,64,64]{2,1,0:T(8,128)S(1)}, u32[]{:S(2)}, u32[]{:S(2)}) collective-permute-start(f32[4,64,64]{2,1,0:T(8,128)S(1)} %bitcast_add_fusion.25), channel_id=1, source_target_pairs={{0,4},{4,12},{12,20},{20,28},{28,24},{24,16},{16,8},{8,0},{1,5},{5... | collective-permute-start | bytes 196616 | tf_op jit(solution)/shard_map/ppermute | solution.py:72
  267.7 5.1 %collective-permute-start.32 = (f32[4,64,64]{2,1,0:T(8,128)S(1)}, f32[4,64,64]{2,1,0:T(8,128)S(1)}, u32[]{:S(2)}, u32[]{:S(2)}) collective-permute-start(f32[4,64,64]{2,1,0:T(8,128)S(1)} %bitcast_add_fusion.17), channel_id=1, source_target_pairs={{0,8},{4,0},{12,4},{20,12},{28,20},{24,28},{16,24},{8,16},{1,9},{5... | collective-permute-start | bytes 196616 | tf_op jit(solution)/shard_map/ppermute | solution.py:72
  268.2 12.2 %collective-permute-start.25 = (f32[4,64,64]{2,1,0:T(8,128)S(1)}, f32[4,64,64]{2,1,0:T(8,128)}, u32[]{:S(2)}, u32[]{:S(2)}) collective-permute-start(f32[4,64,64]{2,1,0:T(8,128)S(1)} %bitcast_add_fusion.24), channel_id=1, source_target_pairs={{0,4},{4,12},{12,20},{20,28},{28,24},{24,16},{16,8},{8,0},{1,5},{5... | collective-permute-start | bytes 196616 | tf_op jit(solution)/shard_map/ppermute | solution.py:72
  273.7 15.1 %collective-permute-start.33 = (f32[4,64,64]{2,1,0:T(8,128)S(1)}, f32[4,64,64]{2,1,0:T(8,128)S(1)}, u32[]{:S(2)}, u32[]{:S(2)}) collective-permute-start(f32[4,64,64]{2,1,0:T(8,128)S(1)} %bitcast_add_fusion.16), channel_id=1, source_target_pairs={{0,8},{4,0},{12,4},{20,12},{28,20},{24,28},{16,24},{8,16},{1,9},{5... | collective-permute-start | bytes 196616 | tf_op jit(solution)/shard_map/ppermute | solution.py:72
  276.2 1.3 copy-start.2
  278.2 40.8 %copy-start.4 = (f32[8,16,16,256]{3,1,0,2:T(8,128)}, f32[8,16,16,256]{3,1,0,2:T(8,128)S(1)}, u32[]{:S(2)}) copy-start(f32[8,16,16,256]{3,1,0,2:T(8,128)S(1)} %get-tuple-element.4) | copy-start | bytes 6291460
  278.2 41.9 %copy-start.3 = (f32[8,16,16,256]{3,1,0,2:T(8,128)}, f32[8,16,16,256]{3,1,0,2:T(8,128)S(1)}, u32[]{:S(2)}) copy-start(f32[8,16,16,256]{3,1,0,2:T(8,128)S(1)} %get-tuple-element.3) | copy-start | bytes 6291460
  278.3 7.7 %collective-permute-start.14 = (f32[16,16,256]{2,0,1:T(8,128)S(1)}, f32[16,16,256]{2,0,1:T(8,128)S(1)}, u32[]{:S(2)}, u32[]{:S(2)}) collective-permute-start(f32[16,16,256]{2,0,1:T(8,128)S(1)} %dynamic-slice_bitcast_fusion), channel_id=1, source_target_pairs={{0,8},{4,0},{12,4},{20,12},{28,20},{24,28},{16,24},{8,16},{1,9},{5... | collective-permute-start | bytes 786440 | tf_op jit(solution)/shard_map/ppermute | solution.py:72
  278.6 8.0 %collective-permute-start.7 = (f32[16,16,256]{2,0,1:T(8,128)S(1)}, f32[16,16,256]{2,0,1:T(8,128)S(1)}, u32[]{:S(2)}, u32[]{:S(2)}) collective-permute-start(f32[16,16,256]{2,0,1:T(8,128)S(1)} %dynamic-slice_bitcast_fusion.1), channel_id=1, source_target_pairs={{0,4},{4,12},{12,20},{20,28},{28,24},{24,16},{16,8},{8,0},{1,5},{5... | collective-permute-start | bytes 786440 | tf_op jit(solution)/shard_map/ppermute | solution.py:72
  281.3 16.6 %collective-permute-start.26 = (f32[4,64,64]{2,1,0:T(8,128)S(1)}, f32[4,64,64]{2,1,0:T(8,128)S(1)}, u32[]{:S(2)}, u32[]{:S(2)}) collective-permute-start(f32[4,64,64]{2,1,0:T(8,128)S(1)} %bitcast_add_fusion.23), channel_id=1, source_target_pairs={{0,4},{4,12},{12,20},{20,28},{28,24},{24,16},{16,8},{8,0},{1,5},{5... | collective-permute-start | bytes 196616 | tf_op jit(solution)/shard_map/ppermute | solution.py:72
  286.0 9.7 %collective-permute-start.15 = (f32[16,16,256]{2,0,1:T(8,128)S(1)}, f32[16,16,256]{2,0,1:T(8,128)S(1)}, u32[]{:S(2)}, u32[]{:S(2)}) collective-permute-start(f32[16,16,256]{2,0,1:T(8,128)S(1)} %bitcast_add_fusion.6), channel_id=1, source_target_pairs={{0,8},{4,0},{12,4},{20,12},{28,20},{24,28},{16,24},{8,16},{1,9},{5... | collective-permute-start | bytes 786440 | tf_op jit(solution)/shard_map/ppermute | solution.py:72
  286.7 9.1 %collective-permute-start.8 = (f32[16,16,256]{2,0,1:T(8,128)S(1)}, f32[16,16,256]{2,0,1:T(8,128)S(1)}, u32[]{:S(2)}, u32[]{:S(2)}) collective-permute-start(f32[16,16,256]{2,0,1:T(8,128)S(1)} %bitcast_add_fusion.13), channel_id=1, source_target_pairs={{0,4},{4,12},{12,20},{20,28},{28,24},{24,16},{16,8},{8,0},{1,5},{5... | collective-permute-start | bytes 786440 | tf_op jit(solution)/shard_map/ppermute | solution.py:72
  289.7 16.8 %collective-permute-start.34 = (f32[4,64,64]{2,1,0:T(8,128)S(1)}, f32[4,64,64]{2,1,0:T(8,128)S(1)}, u32[]{:S(2)}, u32[]{:S(2)}) collective-permute-start(f32[4,64,64]{2,1,0:T(8,128)S(1)} %bitcast_add_fusion.15), channel_id=1, source_target_pairs={{0,8},{4,0},{12,4},{20,12},{28,20},{24,28},{16,24},{8,16},{1,9},{5... | collective-permute-start | bytes 196616 | tf_op jit(solution)/shard_map/ppermute | solution.py:72
  295.8 8.6 %collective-permute-start.16 = (f32[16,16,256]{2,0,1:T(8,128)S(1)}, f32[16,16,256]{2,0,1:T(8,128)S(1)}, u32[]{:S(2)}, u32[]{:S(2)}) collective-permute-start(f32[16,16,256]{2,0,1:T(8,128)S(1)} %bitcast_add_fusion.5), channel_id=1, source_target_pairs={{0,8},{4,0},{12,4},{20,12},{28,20},{24,28},{16,24},{8,16},{1,9},{5... | collective-permute-start | bytes 786440 | tf_op jit(solution)/shard_map/ppermute | solution.py:72
  295.9 8.8 %collective-permute-start.9 = (f32[16,16,256]{2,0,1:T(8,128)S(1)}, f32[16,16,256]{2,0,1:T(8,128)S(1)}, u32[]{:S(2)}, u32[]{:S(2)}) collective-permute-start(f32[16,16,256]{2,0,1:T(8,128)S(1)} %bitcast_add_fusion.12), channel_id=1, source_target_pairs={{0,4},{4,12},{12,20},{20,28},{28,24},{24,16},{16,8},{8,0},{1,5},{5... | collective-permute-start | bytes 786440 | tf_op jit(solution)/shard_map/ppermute | solution.py:72
  298.0 16.4 %collective-permute-start.27 = (f32[4,64,64]{2,1,0:T(8,128)S(1)}, f32[4,64,64]{2,1,0:T(8,128)S(1)}, u32[]{:S(2)}, u32[]{:S(2)}) collective-permute-start(f32[4,64,64]{2,1,0:T(8,128)S(1)} %bitcast_add_fusion.22), channel_id=1, source_target_pairs={{0,4},{4,12},{12,20},{20,28},{28,24},{24,16},{16,8},{8,0},{1,5},{5... | collective-permute-start | bytes 196616 | tf_op jit(solution)/shard_map/ppermute | solution.py:72
  304.4 7.8 %collective-permute-start.17 = (f32[16,16,256]{2,0,1:T(8,128)S(1)}, f32[16,16,256]{2,0,1:T(8,128)S(1)}, u32[]{:S(2)}, u32[]{:S(2)}) collective-permute-start(f32[16,16,256]{2,0,1:T(8,128)S(1)} %bitcast_add_fusion.4), channel_id=1, source_target_pairs={{0,8},{4,0},{12,4},{20,12},{28,20},{24,28},{16,24},{8,16},{1,9},{5... | collective-permute-start | bytes 786440 | tf_op jit(solution)/shard_map/ppermute | solution.py:72
  304.8 8.1 %collective-permute-start.10 = (f32[16,16,256]{2,0,1:T(8,128)S(1)}, f32[16,16,256]{2,0,1:T(8,128)S(1)}, u32[]{:S(2)}, u32[]{:S(2)}) collective-permute-start(f32[16,16,256]{2,0,1:T(8,128)S(1)} %bitcast_add_fusion.11), channel_id=1, source_target_pairs={{0,4},{4,12},{12,20},{20,28},{28,24},{24,16},{16,8},{8,0},{1,5},{5... | collective-permute-start | bytes 786440 | tf_op jit(solution)/shard_map/ppermute | solution.py:72
  312.2 6.9 %collective-permute-start.18 = (f32[16,16,256]{2,0,1:T(8,128)S(1)}, f32[16,16,256]{2,0,1:T(8,128)S(1)}, u32[]{:S(2)}, u32[]{:S(2)}) collective-permute-start(f32[16,16,256]{2,0,1:T(8,128)S(1)} %bitcast_add_fusion.3), channel_id=1, source_target_pairs={{0,8},{4,0},{12,4},{20,12},{28,20},{24,28},{16,24},{8,16},{1,9},{5... | collective-permute-start | bytes 786440 | tf_op jit(solution)/shard_map/ppermute | solution.py:72
  312.9 7.2 %collective-permute-start.11 = (f32[16,16,256]{2,0,1:T(8,128)S(1)}, f32[16,16,256]{2,0,1:T(8,128)S(1)}, u32[]{:S(2)}, u32[]{:S(2)}) collective-permute-start(f32[16,16,256]{2,0,1:T(8,128)S(1)} %bitcast_add_fusion.10), channel_id=1, source_target_pairs={{0,4},{4,12},{12,20},{20,28},{28,24},{24,16},{16,8},{8,0},{1,5},{5... | collective-permute-start | bytes 786440 | tf_op jit(solution)/shard_map/ppermute | solution.py:72
  319.1 6.9 %collective-permute-start.19 = (f32[16,16,256]{2,0,1:T(8,128)S(1)}, f32[16,16,256]{2,0,1:T(8,128)S(1)}, u32[]{:S(2)}, u32[]{:S(2)}) collective-permute-start(f32[16,16,256]{2,0,1:T(8,128)S(1)} %bitcast_add_fusion.2), channel_id=1, source_target_pairs={{0,8},{4,0},{12,4},{20,12},{28,20},{24,28},{16,24},{8,16},{1,9},{5... | collective-permute-start | bytes 786440 | tf_op jit(solution)/shard_map/ppermute | solution.py:72
  320.2 8.2 %collective-permute-start.12 = (f32[16,16,256]{2,0,1:T(8,128)S(1)}, f32[16,16,256]{2,0,1:T(8,128)S(1)}, u32[]{:S(2)}, u32[]{:S(2)}) collective-permute-start(f32[16,16,256]{2,0,1:T(8,128)S(1)} %bitcast_add_fusion.9), channel_id=1, source_target_pairs={{0,4},{4,12},{12,20},{20,28},{28,24},{24,16},{16,8},{8,0},{1,5},{5... | collective-permute-start | bytes 786440 | tf_op jit(solution)/shard_map/ppermute | solution.py:72
  327.0 8.0 %collective-permute-start.20 = (f32[16,16,256]{2,0,1:T(8,128)S(1)}, f32[16,16,256]{2,0,1:T(8,128)S(1)}, u32[]{:S(2)}, u32[]{:S(2)}) collective-permute-start(f32[16,16,256]{2,0,1:T(8,128)S(1)} %bitcast_add_fusion.1), channel_id=1, source_target_pairs={{0,8},{4,0},{12,4},{20,12},{28,20},{24,28},{16,24},{8,16},{1,9},{5... | collective-permute-start | bytes 786440 | tf_op jit(solution)/shard_map/ppermute | solution.py:72
  329.3 6.6 %collective-permute-start.13 = (f32[16,16,256]{2,0,1:T(8,128)S(1)}, f32[16,16,256]{2,0,1:T(8,128)S(1)}, u32[]{:S(2)}, u32[]{:S(2)}) collective-permute-start(f32[16,16,256]{2,0,1:T(8,128)S(1)} %bitcast_add_fusion.8), channel_id=1, source_target_pairs={{0,4},{4,12},{12,20},{20,28},{28,24},{24,16},{16,8},{8,0},{1,5},{5... | collective-permute-start | bytes 786440 | tf_op jit(solution)/shard_map/ppermute | solution.py:72
